TPU v7x, 128 devices: a whole 4x4x4 slice. The times are simulated.
128 devices in a mesh: ang: 64 (over x, y_lo, z, core), pix: 2 (over y_hi).
Axes of the slice: x: 4, y: 4 (y_hi: 2, y_lo: 2; y = y_hi * 2 + y_lo), z: 4, core: 2. Of those that a mesh axis runs over, the one named last changes fastest.
Arguments:
- grads: bfloat16 [2, 4096, 128, 512], P(None, 'ang', 'pix')
- circle_pos: int32 [4096], replicated, may hold values from 0 to 4095, as said below
- harmonics: int32 [256], replicated, may hold values from 0 to 4095, as said below
- support: int32 [128, 512], replicated, may hold values 0 or 1
Outputs:
- update: bfloat16 [2, 4096, 128, 512], P(None, 'ang', 'pix')
- harmonic_rms: float32 [256], replicated
Inputs may be any that keep to these rules, and one draw needn't show every extreme that they name: `circle_pos`: the stored angles form 64 aligned blocks of 64 rows; block b holds the circle positions r_b + 64 * j for j = 0 to 63 in this order, and the 64 values r_b are distinct. `harmonics`: 256 distinct harmonic numbers, among them 0 and 4095.
All inputs are finite; a program needn't handle non-finite values.
Results may differ from a plain program's by a relative error of at most 0.015.
Values may be sent and summed in bfloat16 or wider, within the bound.
No kernel may reach another device: no remote copies, remote signals or barrier semaphores. Data moves between devices by JAX's collectives and lax.ppermute only.
A program may use at most 192 MiB of HBM per device.

v0:
```python
import math
import jax
import jax.numpy as jnp
from jax import lax
from jax.sharding import PartitionSpec as P


def phase_pair(product, modulus):
    radians = (product % modulus).astype(jnp.float32) * (2.0 * math.pi / modulus)
    return (jnp.cos(radians), jnp.sin(radians))


def split_parts(value):
    if value.dtype == jnp.bfloat16:
        return (value,)
    high = value.astype(jnp.bfloat16)
    low = (value - high.astype(jnp.float32)).astype(jnp.bfloat16)
    return (high, low)


def split_einsum(form, left, right):
    left_parts = split_parts(left)
    right_parts = split_parts(right)
    total = None
    for left_rank, left_piece in enumerate(left_parts):
        for right_rank, right_piece in enumerate(right_parts):
            if left_rank + right_rank <= 1:
                term = jnp.einsum(form, left_piece, right_piece, preferred_element_type=jnp.float32)
                total = term if total is None else total + term
    return total


def normalize(coef_re, coef_im, weight, cell_count):
    square_sums = jnp.sum(weight[None, :] * (coef_re * coef_re + coef_im * coef_im), axis=1)
    totals = lax.psum(square_sums, ("ang", "pix"))
    harmonic_rms = jnp.sqrt(totals / cell_count + 1e-06)
    factor = weight[None, :] / harmonic_rms[:, None]
    return (coef_re * factor, coef_im * factor, harmonic_rms)


def direct_path(grads, circle_pos, harmonics, weight, cell_count):
    angle_count = circle_pos.shape[0]
    kept_count = harmonics.shape[0]
    moved = lax.all_to_all(grads, "ang", split_axis=2, concat_axis=1, tiled=True)
    row_local = moved.shape[2]
    col_count = moved.shape[3]
    flat = moved.reshape(2, angle_count, row_local * col_count)
    pixel_count = flat.shape[2]
    phase_cos, phase_sin = phase_pair(harmonics[:, None] * circle_pos[None, :], angle_count)
    table = jnp.concatenate((phase_cos, phase_sin), 0)
    products = split_einsum("ka,ap->kp", table, jnp.concatenate((flat[0], flat[1]), 1))
    scale = 1.0 / math.sqrt(angle_count)
    coef_re = (products[:kept_count, :pixel_count] + products[kept_count:, pixel_count:]) * scale
    coef_im = (products[:kept_count, pixel_count:] - products[kept_count:, :pixel_count]) * scale
    step_re, step_im, harmonic_rms = normalize(coef_re, coef_im, weight, cell_count)
    right_side = jnp.concatenate(
        (jnp.concatenate((step_re, -step_im), 0), jnp.concatenate((step_im, step_re), 0)), 1
    )
    synthesis = split_einsum("ka,kp->ap", table, right_side)
    scale_back = 1.0 / math.sqrt(kept_count)
    update = jnp.stack((synthesis[:, :pixel_count], synthesis[:, pixel_count:])) * scale_back
    update = update.astype(jnp.bfloat16).reshape(2, angle_count, row_local, col_count)
    return (lax.all_to_all(update, "ang", split_axis=1, concat_axis=2, tiled=True), harmonic_rms)


def body(grads, circle_pos, harmonics, support):
    ang_count = lax.axis_size("ang")
    row_pix = grads.shape[2]
    row_local = row_pix // ang_count
    col_count = grads.shape[3]
    row_start = lax.axis_index("pix") * row_pix + lax.axis_index("ang") * row_local
    weight = (
        lax.dynamic_slice_in_dim(support, row_start, row_local, 0).astype(jnp.float32).reshape(-1)
    )
    cell_count = float(row_pix * lax.axis_size("pix") * col_count)
    update, harmonic_rms = direct_path(grads, circle_pos, harmonics, weight, cell_count)
    return (update, harmonic_rms)


def solution(mesh):
    placed = (P(None, "ang", "pix", None), P(), P(), P())
    return jax.shard_map(
        body,
        mesh=mesh,
        in_specs=placed,
        out_specs=(P(None, "ang", "pix", None), P()),
        check_vma=False,
    )
```

profile of v0, /device:TPU:1, one launch (start us, length us, event | category | flops | bytes accessed | tf_op | source)
XLA Modules:
  0.0 437.9 jit_solution(5942899219189294290)
XLA Ops:
  0.6 11.5 %copy.18 = bf16[2,64,64,512]{3,1,0,2:T(8,128)(2,1)} copy(bf16[2,64,64,512]{3,2,1,0:T(8,128)(2,1)} %param.4) | data formatting | bytes 16777216 | tf_op args[0]
  12.1 0.0 copy-start.6
  12.1 0.0 copy-start.8
  12.1 11.2 %all-to-all-start = ((bf16[2,64,64,512]{3,1,0,2:T(8,128)(2,1)}), bf16[2,64,64,512]{3,1,0,2:T(8,128)(2,1)}, u32[]{:S(2)}, u32[]{:S(2)}) async-start(bf16[2,64,64,512]{3,1,0,2:T(8,128)(2,1)} %copy.18), calls=%async_computation | async-start | bytes 16777216 | tf_op jit(solution)/shard_map/all_to_all | solution.py:44
  23.3 0.7 dynamic-slice_convert_fusion
  24.1 0.0 copy-done.6
  24.1 0.0 copy-done.8
  24.1 18.0 %fusion.8 = (f32[256,4096]{1,0:T(8,128)}, f32[256,4096]{1,0:T(8,128)}) fusion(s32[4096]{0:T(1024)S(1)} %copy-done.6, s32[256]{0:T(256)S(1)} %copy-done.8), kind=kLoop, calls=%fused_computation.23 | loop fusion | flops 14680064 | bytes 8406016 | tf_op jit(solution)/shard_map/cos | solution.py:10
  42.1 84.6 %all-to-all-done = bf16[2,64,64,512]{3,1,0,2:T(8,128)(2,1)} async-done(((bf16[2,64,64,512]{3,1,0,2:T(8,128)(2,1)}), bf16[2,64,64,512]{3,1,0,2:T(8,128)(2,1)}, u32[]{:S(2)}, u32[]{:S(2)}) %all-to-all-start) | async-done | bytes 8388640 | tf_op jit(solution)/shard_map/all_to_all | solution.py:44
  126.7 7.9 %copy.24 = bf16[2,64,64,512]{3,1,2,0:T(8,128)(2,1)} copy(bf16[2,64,64,512]{3,1,0,2:T(8,128)(2,1)} %all-to-all-done) | data formatting | bytes 16777216 | tf_op jit(solution)/shard_map/all_to_all | solution.py:44
  134.6 0.0 copy-start
  134.6 0.0 copy-start.2
  134.6 5.4 %fusion.27 = (bf16[1,64,64,1,512]{4,2,1,3,0:T(8,128)(2,1)S(1)}, bf16[1,64,64,1,512]{4,2,1,3,0:T(8,128)(2,1)}) fusion(bf16[2,64,64,1,512]{4,2,1,3,0:T(8,128)(2,1)} %bitcast.17), kind=kLoop, calls=%fused_computation.41 | loop fusion | bytes 16777216 | tf_op jit(solution)/shard_map/slice | solution.py:51
  140.0 0.0 copy-start.5
  140.0 2.1 copy-done.5
  142.1 0.0 copy-done
  142.1 1.5 copy-done.2
  143.6 8.0 %fusion.2 = f32[512,1024]{1,0:T(8,128)} fusion(bf16[4096,512]{1,0:T(8,128)(2,1)} %bitcast.21, bf16[4096,512]{1,0:T(8,128)(2,1)S(1)} %bitcast.19, f32[256,4096]{1,0:T(8,128)S(1)} %copy-done.2, f32[256,4096]{1,0:T(8,128)S(1)} %copy-done), kind=kOutput, calls=%fused_computation.15 | convolution fusion | flops 4322230272 | bytes 18874368 | tf_op jit(solution)/shard_map/ka,ap->kp/dot_general | solution.py:28
  151.6 8.5 %fusion.9 = f32[512,1024]{1,0:T(8,128)S(1)} fusion(f32[512,1024]{1,0:T(8,128)} %fusion.2, bf16[4096,512]{1,0:T(8,128)(2,1)} %bitcast.22, bf16[4096,512]{1,0:T(8,128)(2,1)} %bitcast.20, f32[256,4096]{1,0:T(8,128)S(1)} %copy-done.2, f32[256,4096]{1,0:T(8,128)S(1)} %copy-done), kind=kOutput, calls=%fused_computation.24 | convolution fusion | flops 4320657408 | bytes 20971520 | tf_op jit(solution)/shard_map/ka,ap->kp/dot_general | solution.py:28
  160.1 0.0 copy-start.4
  160.2 1.3 copy-done.4
  161.5 0.2 multiply_reduce_fusion
  161.7 70.5 %psum.7 = f32[256]{0:T(256)S(1)} all-reduce(f32[256]{0:T(256)S(1)} %multiply_reduce_fusion), channel_id=1, replica_groups=mesh['ang'=64,'pix'=2] {'ang','pix'}, use_global_device_ids=true, to_apply=%region_1.2 | all-reduce | flops 256 | bytes 2048 | tf_op jit(solution)/shard_map/psum | solution.py:35
  232.2 0.0 copy-start.7
  232.3 1.7 fusion.26
  234.0 0.0 copy-start.1
  234.0 0.0 copy-start.3
  234.0 12.7 %fusion.11 = f32[4096,1024]{1,0:T(8,128)} fusion(f32[256,512]{1,0:T(8,128)S(1)} %get-tuple-element.12, f32[256,512]{1,0:T(8,128)S(1)} %get-tuple-element.7, f32[256,512]{1,0:T(8,128)S(1)} %get-tuple-element.6, f32[256,4096]{1,0:T(8,128)} %get-tuple-element.14, f32[256,4096]{1,0:T(8,128)} %get-tuple-element.13), kind=kOutput, calls=%fused_computation.26 | convolution fusion | flops 4307025920 | bytes 26738688 | tf_op jit(solution)/shard_map/ka,kp->ap/dot_general | solution.py:28
  246.7 0.0 copy-done.7
  246.7 0.0 copy-done.1
  246.7 0.0 copy-done.3
  246.7 8.2 %fusion.19 = f32[4096,1024]{1,0:T(8,128)} fusion(f32[256,512]{1,0:T(8,128)S(1)} %get-tuple-element.12, f32[256,512]{1,0:T(8,128)S(1)} %get-tuple-element.7, f32[256,512]{1,0:T(8,128)S(1)} %get-tuple-element.6, f32[256,4096]{1,0:T(8,128)S(1)} %copy-done.3, f32[256,4096]{1,0:T(8,128)S(1)} %copy-done.1), kind=kOutput, calls=%fused_computation.39 | convolution fusion | flops 4307550208 | bytes 26738688 | tf_op jit(solution)/shard_map/ka,kp->ap/dot_general | solution.py:28
  254.9 19.3 %add_add_fusion = f32[4096,1024]{1,0:T(8,128)} fusion(f32[4096,1024]{1,0:T(8,128)} %fusion.19, f32[4096,1024]{1,0:T(8,128)} %fusion.11, f32[256,512]{1,0:T(8,128)S(1)} %get-tuple-element.12, f32[256,512]{1,0:T(8,128)S(1)} %get-tuple-element.7, f32[256,512]{1,0:T(8,128)S(1)} %get-tuple-element.6, f32[256,4096]{1,0:T(8,128)} %get-tuple-element.14, ...), kind=kOutput, calls=%fused_computation.2 | convolution fusion | flops 4318035968 | bytes 60293120 | tf_op jit(solution)/shard_map/ka,kp->ap/dot_general | solution.py:28
  274.1 6.9 %slice_bitcast_fusion.1 = (f32[1,4096,1,512]{3,1,2,0:T(8,128)S(1)}, f32[1,4096,1,512]{3,1,2,0:T(8,128)S(1)}) fusion(f32[4096,1024]{1,0:T(8,128)} %add_add_fusion), kind=kLoop, calls=%fused_computation.4 | loop fusion | bytes 33554432 | tf_op jit(solution)/shard_map/stack | solution.py:61
  281.0 2.5 fusion
  283.5 32.6 %copy.20 = bf16[2,4096,1,512]{3,0,2,1:T(2,128)(2,1)S(1)} copy(bf16[2,4096,1,512]{3,1,2,0:T(8,128)(2,1)S(1)} %fusion) | data formatting | bytes 16777216 | tf_op jit(solution)/shard_map/convert_element_type | solution.py:62
  316.2 102.3 %all_to_all.33 = bf16[2,4096,1,512]{3,0,2,1:T(2,128)(2,1)} all-to-all(bf16[2,4096,1,512]{3,0,2,1:T(2,128)(2,1)S(1)} %copy.20), channel_id=1, replica_groups=mesh['ang'=64,'pix'=2] {'ang'}, dimensions={1} | all-to-all | bytes 16777216 | tf_op jit(solution)/shard_map/all_to_all | solution.py:63
  418.4 8.0 %copy.21 = bf16[2,4096,1,512]{3,1,0,2:T(8,128)(2,1)} copy(bf16[2,4096,1,512]{3,0,2,1:T(2,128)(2,1)} %all_to_all.33) | data formatting | bytes 16777216 | tf_op jit(solution)/shard_map/all_to_all | solution.py:63
  426.4 11.5 %copy.22 = bf16[2,64,64,512]{3,2,1,0:T(8,128)(2,1)} copy(bf16[2,64,64,512]{3,1,2,0:T(8,128)(2,1)} %bitcast.18) | data formatting | bytes 16777216
  (1 shorter events, 0.0 us)
Async XLA Ops:
  12.1 11.9 %copy-start.6 = (s32[4096]{0:T(1024)S(1)}, s32[4096]{0:T(1024)}, u32[]{:S(2)}) copy-start(s32[4096]{0:T(1024)} %param.5) | copy-start | bytes 49156
  12.1 11.9 %copy-start.8 = (s32[256]{0:T(256)S(1)}, s32[256]{0:T(256)}, u32[]{:S(2)}) copy-start(s32[256]{0:T(256)} %param.6) | copy-start | bytes 3076
  12.1 114.6 %all-to-all-start = ((bf16[2,64,64,512]{3,1,0,2:T(8,128)(2,1)}), bf16[2,64,64,512]{3,1,0,2:T(8,128)(2,1)}, u32[]{:S(2)}, u32[]{:S(2)}) async-start(bf16[2,64,64,512]{3,1,0,2:T(8,128)(2,1)} %copy.18), calls=%async_computation | async-start | bytes 16777216 | tf_op jit(solution)/shard_map/all_to_all | solution.py:44
  134.6 7.5 %copy-start = (f32[256,4096]{1,0:T(8,128)S(1)}, f32[256,4096]{1,0:T(8,128)}, u32[]{:S(2)}) copy-start(f32[256,4096]{1,0:T(8,128)} %get-tuple-element.13) | copy-start | bytes 12582916
  134.6 9.0 %copy-start.2 = (f32[256,4096]{1,0:T(8,128)S(1)}, f32[256,4096]{1,0:T(8,128)}, u32[]{:S(2)}) copy-start(f32[256,4096]{1,0:T(8,128)} %get-tuple-element.14) | copy-start | bytes 12582916
  140.0 2.1 copy-start.5
  160.1 1.3 copy-start.4
  232.2 14.4 %copy-start.7 = (f32[256]{0:T(256)}, f32[256]{0:T(256)S(1)}, u32[]{:S(2)}) copy-start(f32[256]{0:T(256)S(1)} %add_sqrt_fusion) | copy-start | bytes 3076
  234.0 12.7 %copy-start.1 = (f32[256,4096]{1,0:T(8,128)S(1)}, f32[256,4096]{1,0:T(8,128)}, u32[]{:S(2)}) copy-start(f32[256,4096]{1,0:T(8,128)} %get-tuple-element.13) | copy-start | bytes 12582916
  234.0 12.7 %copy-start.3 = (f32[256,4096]{1,0:T(8,128)S(1)}, f32[256,4096]{1,0:T(8,128)}, u32[]{:S(2)}) copy-start(f32[256,4096]{1,0:T(8,128)} %get-tuple-element.14) | copy-start | bytes 12582916
where the time goes:
time: 438 us
  blocking collectives  173 us (39%)
  local copies, waits for them, and re-layouts  88.7 us (20%)
  waiting for transfers between devices  84.6 us (19%)
  matrix products  56.7 us (13%)
  other arithmetic  23.2 us (5%)
  starting transfers between devices  11.2 us (3%)
    all_to_all x1, blocking collectives, direct_path(): lax.all_to_all(update, 'ang', split_axis=1, concat_axis=2, tiled=True)  102 us
    all_to_all x1, waiting for transfers between devices, direct_path(): lax.all_to_all(grads, 'ang', split_axis=2, concat_axis=1, tiled=True)  84.6 us
    psum x1, blocking collectives, normalize(): totals = lax.psum(square_sums, ('ang', 'pix'))  70.5 us
    dot_general x5, matrix products, split_einsum(): jnp.einsum(form, left_piece, right_piece, preferred_element_type=jnp.floa...  56.7 us
    convert_element_type x1, local copies, waits for them, and re-layouts, direct_path(): update.astype(jnp.bfloat16).reshape(2, angle_count, row_local, col_count)  32.6 us
    unnamed x20, local copies, waits for them, and re-layouts  28 us
    cos x1, other arithmetic, phase_pair(): return (jnp.cos(radians), jnp.sin(radians))  18 us
    all_to_all x1, starting transfers between devices, direct_path(): lax.all_to_all(grads, 'ang', split_axis=2, concat_axis=1, tiled=True)  11.2 us
  transfers between devices with their start and end apart: 1, of which 1 were waited for; matrix products, arithmetic and copies ran while one was open for 4% of the time, Pallas kernels for 0%

commit v1 on v0

--- a/solution.py
+++ b/solution.py
@@ -1,8 +1,17 @@
+import functools
 import math
 import jax
 import jax.numpy as jnp
 from jax import lax
 from jax.sharding import PartitionSpec as P
+from jax.lax import all_gather
+
+
+def _resolve_meshes(sample, mesh_dim):
+    return jnp.sum(all_gather(sample, axis_name=mesh_dim), axis=0)
+
+
+series_all_define = functools.partial(_resolve_meshes, mesh_dim=("ang", "pix"))
 
 
 def phase_pair(product, modulus):
@@ -32,7 +41,7 @@
 
 def normalize(coef_re, coef_im, weight, cell_count):
     square_sums = jnp.sum(weight[None, :] * (coef_re * coef_re + coef_im * coef_im), axis=1)
-    totals = lax.psum(square_sums, ("ang", "pix"))
+    totals = series_all_define(square_sums)
     harmonic_rms = jnp.sqrt(totals / cell_count + 1e-06)
     factor = weight[None, :] / harmonic_rms[:, None]
     return (coef_re * factor, coef_im * factor, harmonic_rms)

time: 438 us -> 688 us (1.57)
  blocking collectives: 173 us -> 422 us
    all_gather x0 -> x1, blocking collectives: none -> 318 us  [_resolve_meshes(): return jnp.sum(all_gather(sample, axis_name=mesh_dim), axis=0)]
    psum x1 -> x0, blocking collectives: 70.5 us -> none  [normalize(): totals = lax.psum(square_sums, ('ang', 'pix'))]
  transfers between devices with their start and end apart: 1 -> 1, of which waited for: 1 -> 1; matrix products, arithmetic and copies ran while one was open for 4% -> 3% of each run, Pallas kernels for 0% -> 0%
where the time goes in v1:
time: 688 us; the launch traced here: 687 us
  blocking collectives  422 us (61%)
  local copies, waits for them, and re-layouts  88.7 us (13%)
  waiting for transfers between devices  84.6 us (12%)
  matrix products  56.7 us (8%)
  other arithmetic  23.4 us (3%)
  starting transfers between devices  11.2 us (2%)
    all_gather x1, blocking collectives, _resolve_meshes(): return jnp.sum(all_gather(sample, axis_name=mesh_dim), axis=0)  318 us
    all_to_all x1, blocking collectives, direct_path(): lax.all_to_all(update, 'ang', split_axis=1, concat_axis=2, tiled=True)  104 us
    all_to_all x1, waiting for transfers between devices, direct_path(): lax.all_to_all(grads, 'ang', split_axis=2, concat_axis=1, tiled=True)  84.6 us
    dot_general x5, matrix products, split_einsum(): jnp.einsum(form, left_piece, right_piece, preferred_element_type=jnp.floa...  56.7 us
    convert_element_type x1, local copies, waits for them, and re-layouts, direct_path(): update.astype(jnp.bfloat16).reshape(2, angle_count, row_local, col_count)  32.6 us
    unnamed x20, local copies, waits for them, and re-layouts  28 us
    cos x1, other arithmetic, phase_pair(): return (jnp.cos(radians), jnp.sin(radians))  18 us
  transfers between devices with their start and end apart: 1, of which 1 were waited for; matrix products, arithmetic and copies ran while one was open for 3% of the time, Pallas kernels for 0%

profile of v1, /device:TPU:1, one launch (start us, length us, event | category | flops | bytes accessed | tf_op | source)
XLA Modules:
  0.0 687.3 jit_solution(5113141207960427377)
XLA Ops:
  0.6 11.5 %copy.18 = bf16[2,64,64,512]{3,1,0,2:T(8,128)(2,1)} copy(bf16[2,64,64,512]{3,2,1,0:T(8,128)(2,1)} %param.4) | data formatting | bytes 16777216 | tf_op args[0]
  12.1 0.0 copy-start.6
  12.1 0.0 copy-start.8
  12.1 11.2 %all-to-all-start = ((bf16[2,64,64,512]{3,1,0,2:T(8,128)(2,1)}), bf16[2,64,64,512]{3,1,0,2:T(8,128)(2,1)}, u32[]{:S(2)}, u32[]{:S(2)}) async-start(bf16[2,64,64,512]{3,1,0,2:T(8,128)(2,1)} %copy.18), calls=%async_computation | async-start | bytes 16777216 | tf_op jit(solution)/shard_map/all_to_all | solution.py:53
  23.3 0.7 dynamic-slice_convert_fusion
  24.1 0.0 copy-done.6
  24.1 0.0 copy-done.8
  24.1 18.0 %fusion.8 = (f32[256,4096]{1,0:T(8,128)}, f32[256,4096]{1,0:T(8,128)}) fusion(s32[4096]{0:T(1024)S(1)} %copy-done.6, s32[256]{0:T(256)S(1)} %copy-done.8), kind=kLoop, calls=%fused_computation.23 | loop fusion | flops 14680064 | bytes 8406016 | tf_op jit(solution)/shard_map/cos | solution.py:19
  42.1 84.6 %all-to-all-done = bf16[2,64,64,512]{3,1,0,2:T(8,128)(2,1)} async-done(((bf16[2,64,64,512]{3,1,0,2:T(8,128)(2,1)}), bf16[2,64,64,512]{3,1,0,2:T(8,128)(2,1)}, u32[]{:S(2)}, u32[]{:S(2)}) %all-to-all-start) | async-done | bytes 8388640 | tf_op jit(solution)/shard_map/all_to_all | solution.py:53
  126.7 7.9 %copy.24 = bf16[2,64,64,512]{3,1,2,0:T(8,128)(2,1)} copy(bf16[2,64,64,512]{3,1,0,2:T(8,128)(2,1)} %all-to-all-done) | data formatting | bytes 16777216 | tf_op jit(solution)/shard_map/all_to_all | solution.py:53
  134.6 0.0 copy-start
  134.6 0.0 copy-start.2
  134.6 5.4 fusion.27
  140.0 0.0 copy-start.5
  140.0 2.1 copy-done.5
  142.1 0.0 copy-done
  142.1 1.5 copy-done.2
  143.6 8.0 %fusion.2 = f32[512,1024]{1,0:T(8,128)} fusion(bf16[4096,512]{1,0:T(8,128)(2,1)} %bitcast.22, bf16[4096,512]{1,0:T(8,128)(2,1)S(1)} %bitcast.20, f32[256,4096]{1,0:T(8,128)S(1)} %copy-done.2, f32[256,4096]{1,0:T(8,128)S(1)} %copy-done), kind=kOutput, calls=%fused_computation.15 | convolution fusion | flops 4322230272 | bytes 18874368 | tf_op jit(solution)/shard_map/ka,ap->kp/dot_general | solution.py:37
  151.6 8.5 %fusion.9 = f32[512,1024]{1,0:T(8,128)S(1)} fusion(f32[512,1024]{1,0:T(8,128)} %fusion.2, bf16[4096,512]{1,0:T(8,128)(2,1)} %bitcast.23, bf16[4096,512]{1,0:T(8,128)(2,1)} %bitcast.21, f32[256,4096]{1,0:T(8,128)S(1)} %copy-done.2, f32[256,4096]{1,0:T(8,128)S(1)} %copy-done), kind=kOutput, calls=%fused_computation.24 | convolution fusion | flops 4320657408 | bytes 20971520 | tf_op jit(solution)/shard_map/ka,ap->kp/dot_general | solution.py:37
  160.1 0.0 copy-start.4
  160.2 1.3 copy-done.4
  161.5 0.2 multiply_reduce_fusion
  161.7 317.8 %all-gather.1 = f32[128,1,256]{2,1,0:T(1,128)S(1)} all-gather(f32[1,1,256]{2,1,0:T(1,128)S(1)} %bitcast.26), channel_id=2, replica_groups=mesh['ang'=64,'pix'=2] {'ang','pix'}, dimensions={0}, use_global_device_ids=true | all-gather | bytes 132096 | tf_op jit(solution)/shard_map/all_gather | solution.py:11
  479.5 0.2 reduce_sum.19
  479.6 0.0 copy-start.7
  479.6 1.7 fusion.26
  481.4 0.0 copy-start.1
  481.4 0.0 copy-start.3
  481.4 12.7 %fusion.11 = f32[4096,1024]{1,0:T(8,128)} fusion(f32[256,512]{1,0:T(8,128)S(1)} %get-tuple-element.12, f32[256,512]{1,0:T(8,128)S(1)} %get-tuple-element.7, f32[256,512]{1,0:T(8,128)S(1)} %get-tuple-element.6, f32[256,4096]{1,0:T(8,128)} %get-tuple-element.14, f32[256,4096]{1,0:T(8,128)} %get-tuple-element.13), kind=kOutput, calls=%fused_computation.26 | convolution fusion | flops 4307025920 | bytes 26738688 | tf_op jit(solution)/shard_map/ka,kp->ap/dot_general | solution.py:37
  494.1 0.0 copy-done.7
  494.1 0.0 copy-done.1
  494.1 0.0 copy-done.3
  494.1 8.2 %fusion.19 = f32[4096,1024]{1,0:T(8,128)} fusion(f32[256,512]{1,0:T(8,128)S(1)} %get-tuple-element.12, f32[256,512]{1,0:T(8,128)S(1)} %get-tuple-element.7, f32[256,512]{1,0:T(8,128)S(1)} %get-tuple-element.6, f32[256,4096]{1,0:T(8,128)S(1)} %copy-done.3, f32[256,4096]{1,0:T(8,128)S(1)} %copy-done.1), kind=kOutput, calls=%fused_computation.39 | convolution fusion | flops 4307550208 | bytes 26738688 | tf_op jit(solution)/shard_map/ka,kp->ap/dot_general | solution.py:37
  502.2 19.3 %add_add_fusion = f32[4096,1024]{1,0:T(8,128)} fusion(f32[4096,1024]{1,0:T(8,128)} %fusion.19, f32[4096,1024]{1,0:T(8,128)} %fusion.11, f32[256,512]{1,0:T(8,128)S(1)} %get-tuple-element.12, f32[256,512]{1,0:T(8,128)S(1)} %get-tuple-element.7, f32[256,512]{1,0:T(8,128)S(1)} %get-tuple-element.6, f32[256,4096]{1,0:T(8,128)} %get-tuple-element.14, ...), kind=kOutput, calls=%fused_computation.2 | convolution fusion | flops 4318035968 | bytes 60293120 | tf_op jit(solution)/shard_map/ka,kp->ap/dot_general | solution.py:37
  521.5 6.9 slice_bitcast_fusion.1
  528.4 2.5 fusion
  530.9 32.6 %copy.20 = bf16[2,4096,1,512]{3,0,2,1:T(2,128)(2,1)S(1)} copy(bf16[2,4096,1,512]{3,1,2,0:T(8,128)(2,1)S(1)} %fusion) | data formatting | bytes 16777216 | tf_op jit(solution)/shard_map/convert_element_type | solution.py:71
  563.5 104.3 %all_to_all.33 = bf16[2,4096,1,512]{3,0,2,1:T(2,128)(2,1)} all-to-all(bf16[2,4096,1,512]{3,0,2,1:T(2,128)(2,1)S(1)} %copy.20), channel_id=1, replica_groups=mesh['ang'=64,'pix'=2] {'ang'}, dimensions={1} | all-to-all | bytes 16777216 | tf_op jit(solution)/shard_map/all_to_all | solution.py:72
  667.8 8.0 %copy.21 = bf16[2,4096,1,512]{3,1,0,2:T(8,128)(2,1)} copy(bf16[2,4096,1,512]{3,0,2,1:T(2,128)(2,1)} %all_to_all.33) | data formatting | bytes 16777216 | tf_op jit(solution)/shard_map/all_to_all | solution.py:72
  675.8 11.5 %copy.22 = bf16[2,64,64,512]{3,2,1,0:T(8,128)(2,1)} copy(bf16[2,64,64,512]{3,1,2,0:T(8,128)(2,1)} %bitcast.19) | data formatting | bytes 16777216
  (1 shorter events, 0.0 us)
Async XLA Ops:
  12.1 11.9 %copy-start.6 = (s32[4096]{0:T(1024)S(1)}, s32[4096]{0:T(1024)}, u32[]{:S(2)}) copy-start(s32[4096]{0:T(1024)} %param.5) | copy-start | bytes 49156
  12.1 11.9 %copy-start.8 = (s32[256]{0:T(256)S(1)}, s32[256]{0:T(256)}, u32[]{:S(2)}) copy-start(s32[256]{0:T(256)} %param.6) | copy-start | bytes 3076
  12.1 114.6 %all-to-all-start = ((bf16[2,64,64,512]{3,1,0,2:T(8,128)(2,1)}), bf16[2,64,64,512]{3,1,0,2:T(8,128)(2,1)}, u32[]{:S(2)}, u32[]{:S(2)}) async-start(bf16[2,64,64,512]{3,1,0,2:T(8,128)(2,1)} %copy.18), calls=%async_computation | async-start | bytes 16777216 | tf_op jit(solution)/shard_map/all_to_all | solution.py:53
  134.6 7.5 %copy-start = (f32[256,4096]{1,0:T(8,128)S(1)}, f32[256,4096]{1,0:T(8,128)}, u32[]{:S(2)}) copy-start(f32[256,4096]{1,0:T(8,128)} %get-tuple-element.13) | copy-start | bytes 12582916
  134.6 9.0 %copy-start.2 = (f32[256,4096]{1,0:T(8,128)S(1)}, f32[256,4096]{1,0:T(8,128)}, u32[]{:S(2)}) copy-start(f32[256,4096]{1,0:T(8,128)} %get-tuple-element.14) | copy-start | bytes 12582916
  140.0 2.1 copy-start.5
  160.1 1.3 copy-start.4
  479.6 14.4 %copy-start.7 = (f32[256]{0:T(256)}, f32[256]{0:T(256)S(1)}, u32[]{:S(2)}) copy-start(f32[256]{0:T(256)S(1)} %add_sqrt_fusion) | copy-start | bytes 3076
  481.4 12.7 %copy-start.1 = (f32[256,4096]{1,0:T(8,128)S(1)}, f32[256,4096]{1,0:T(8,128)}, u32[]{:S(2)}) copy-start(f32[256,4096]{1,0:T(8,128)} %get-tuple-element.13) | copy-start | bytes 12582916
  481.4 12.7 %copy-start.3 = (f32[256,4096]{1,0:T(8,128)S(1)}, f32[256,4096]{1,0:T(8,128)}, u32[]{:S(2)}) copy-start(f32[256,4096]{1,0:T(8,128)} %get-tuple-element.14) | copy-start | bytes 12582916
